TPU v7x, 32 devices: a whole 2x2x4 slice. The times are simulated.
32 devices in a mesh: row: 4 (over y, x), col: 4 (over z), pts: 2 (over core).
Axes of the slice: x: 2, y: 2, z: 4, core: 2. Of those that a mesh axis runs over, the one named last changes fastest.
Arguments:
- green_panel: bfloat16 [4, 2, 512, 6144], P(None, None, 'col', 'pts'), may hold values from -6 to 6
- log_psd: float32 [2, 4, 3072], P('pts', None, ('row', 'col')), may hold values from -1.1 to 1.1
- observed: float32 [4, 2, 512, 512], P(None, None, 'row', 'col'), may hold values from -1 to 1
- pair_weights: int32 [512, 512], P('row', 'col'), may hold values from 0 to 4, as said below
Outputs:
- updated_log_psd: float32 [2, 4, 3072], P('pts', None, ('row', 'col'))
Inputs may be any that keep to these rules, and one draw needn't show every extreme that they name: pair_weights is 0 for pairs that are not listed and for every station paired with itself; the share of listed pairs differs from one block of 128 x 128 pairs (one index of row by one of col) to another, and some such blocks list no pair.
All inputs are finite; a program needn't handle non-finite values.
Results may differ from a plain program's by a relative error of at most 0.0014.
Values may be sent and summed in bfloat16 or wider, within the bound.
No kernel may reach another device: no remote copies, remote signals or barrier semaphores. Data moves between devices by JAX's collectives and lax.ppermute only.
A program may use at most 64 MiB of HBM per device.

v0:
```python
import jax
import jax.numpy as jnp
from jax import lax
from jax.sharding import PartitionSpec as P

ITERS = 2
epsilon = 1e-06
descent = 0.1


def from_root(block, axis, source):
    block = jnp.where(lax.axis_index(axis) == source, block, jnp.zeros_like(block))
    return lax.psum(block, axis)


def pair_total(partial_value):
    return lax.psum(partial_value.astype(jnp.bfloat16), "pts").astype(jnp.float32)


def descend(log_field, gradient, entry_count):
    squares = lax.psum(jnp.sum(gradient * gradient), ("row", "col", "pts"))
    return log_field - descent * gradient / jnp.sqrt(squares / entry_count + epsilon)


def correlate(left_rows, weighted):
    half_a = left_rows.shape[1] // 2
    half_b = weighted.shape[1] // 2
    products = jnp.einsum("fan,fbn->fab", left_rows, weighted, preferred_element_type=jnp.float32)
    corr_real = products[:, :half_a, :half_b] + products[:, half_a:, half_b:]
    corr_imag = products[:, half_a:, :half_b] - products[:, :half_a, half_b:]
    return jnp.stack([corr_real, corr_imag], axis=1)


def adjoint_block(adjoint):
    adj_real = adjoint[:, 0]
    adj_imag = adjoint[:, 1]
    top_half = jnp.concatenate([adj_real, -adj_imag], axis=2)
    low_half = jnp.concatenate([adj_imag, adj_real], axis=2)
    return jnp.concatenate([top_half, low_half], axis=1)


def point_terms(adjoint, right_rows, left_rows, psd_field, quad_weight):
    accumulated = jnp.einsum(
        "fab,fbn->fan", adjoint_block(adjoint), right_rows, preferred_element_type=jnp.float32
    )
    return quad_weight * psd_field * jnp.sum(left_rows * accumulated, axis=1)


def body(green_panel, log_psd, observed, pair_weights):
    freq_count, comp_count, span_j, local_pts = green_panel.shape
    span_i = observed.shape[2]
    row_count = lax.axis_size("row")
    col_count = lax.axis_size("col")
    pts_count = lax.axis_size("pts")
    quad_weight = 1.0 / (pts_count * local_pts)
    entry_count = freq_count * pts_count * local_pts
    pair_scale = pair_weights.astype(jnp.float32)
    log_start = log_psd[0]
    group_ratio = col_count // row_count
    pieces = []
    for member in range(group_ratio):
        pieces.append(from_root(green_panel, "col", lax.axis_index("row") * group_ratio + member))
    rows_block = jnp.concatenate(pieces, axis=2).reshape(freq_count, 2 * span_i, local_pts)
    cols_block = green_panel.reshape(freq_count, 2 * span_j, local_pts)

    def run_sweep(sweep_idx, log_field):
        whole_log = lax.all_gather(log_field, ("row", "col"), axis=1, tiled=True)
        psd_field = jnp.exp(whole_log)
        weighted = (green_panel * psd_field[:, None, None, :]).astype(jnp.bfloat16)
        weighted = weighted.reshape(freq_count, 2 * span_j, local_pts)
        partial_value = correlate(rows_block, weighted)
        pair_sum = pair_total(partial_value)
        adjoint = (pair_scale * (quad_weight * pair_sum - observed)).astype(jnp.bfloat16)
        point_part = point_terms(adjoint, cols_block, rows_block, psd_field, quad_weight)
        gradient = lax.psum_scatter(point_part, ("row", "col"), scatter_dimension=1, tiled=True)
        return descend(log_field, gradient, entry_count)

    log_final = lax.fori_loop(0, ITERS, run_sweep, log_start)
    return log_final[None]


def solution(mesh):
    return jax.shard_map(
        body,
        mesh=mesh,
        in_specs=(
            P(None, None, "col", "pts"),
            P("pts", None, ("row", "col")),
            P(None, None, "row", "col"),
            P("row", "col"),
        ),
        out_specs=P("pts", None, ("row", "col")),
        check_vma=False,
    )
```

profile of v0, /device:TPU:0, one launch (start us, length us, event | category | flops | bytes accessed | tf_op | source)
XLA Modules:
  0.0 727.3 jit_solution(13803645193533125202)
XLA Ops:
  6.5 5.8 broadcast_select_fusion
  12.4 1.0 copy-done
  13.8 224.4 %all-reduce.3.cloned.1.call-done = bf16[4,256,3072]{2,1,0:T(8,128)(2,1)} async-done(((bf16[4,256,3072]{2,1,0:T(8,128)(2,1)}), bf16[4,256,3072]{2,1,0:T(8,128)(2,1)}) %all-reduce.3.cloned.1.call-update) | async-done | bytes 6291472 | tf_op jit(solution)/shard_map/psum | solution.py:13
  238.1 482.1 %while.10 = (s32[]{:T(128)}, f32[4,192]{1,0:T(4,128)S(1)}, bf16[4,256,3072]{2,1,0:T(8,128)(2,1)}, f32[128,128]{0,1:T(8,128)S(1)}, bf16[4,2,128,3072]{3,2,1,0:T(8...) while((s32[]{:T(128)}, f32[4,192]{1,0:T(4,128)S(1)}, ...), condition=%wide.region_7.8_spmd, body=%wide.region_1.7_spmd.sunk | while | flops 3243458304 | bytes 34303204 | solution.py:78
  238.2 39.0 %all-gather.2 = f32[16,192,4]{1,2,0:T(4,128)S(1)} all-gather(f32[1,192,4]{1,2,0:T(4,128)S(1)} %bitcast.59), channel_id=1, replica_groups=mesh['row'=4,'col'=4,'pts'=2] {'row','col'}, dimensions={0}, use_global_device_ids=true | all-gather | bytes 52224 | tf_op jit(solution)/shard_map/while/body/eval_jaxpr/all_gather | solution.py:67
  277.2 6.4 fusion.33
  283.7 0.7 pad_maximum_fusion.2
  284.6 14.6 %all-reduce.5.cloned.1.call-done = bf16[4,2,128,128]{2,3,0,1:T(8,128)(2,1)} async-done(((bf16[4,2,128,128]{2,3,0,1:T(8,128)(2,1)}), bf16[4,2,128,128]{2,3,0,1:T(8,128)(2,1)}) %all-reduce.5.cloned.1.call-update) | async-done | bytes 262160 | tf_op jit(solution)/shard_map/while/body/eval_jaxpr/psum | solution.py:17
  299.2 1.0 multiply_convert_fusion.2
  300.3 6.8 multiply_reduce_fusion.4
  307.1 1.7 copy.28
  308.8 127.5 %reduce-scatter.6.cloned.1.call-done = f32[192,4]{1,0:T(8,128)} async-done(((f32[3072,4]{1,0:T(8,128)}), f32[192,4]{1,0:T(8,128)}) %reduce-scatter.6.cloned.1.call-update) | async-done | bytes 3088 | tf_op jit(solution)/shard_map/while
  436.3 1.0 copy.29
  437.9 40.0 %psum.25 = f32[]{:T(128)} all-reduce(f32[]{:T(128)} %multiply_reduce_fusion.5), channel_id=1, replica_groups=mesh['row'=4,'col'=4,'pts'=2] {'row','col','pts'}, use_global_device_ids=true, to_apply=%region_6.6 | all-reduce | flops 1 | bytes 8 | tf_op jit(solution)/shard_map/while/body/eval_jaxpr/psum | solution.py:21
  478.6 39.4 %all-gather.2 = f32[16,192,4]{1,2,0:T(4,128)S(1)} all-gather(f32[1,192,4]{1,2,0:T(4,128)S(1)} %bitcast.59), channel_id=1, replica_groups=mesh['row'=4,'col'=4,'pts'=2] {'row','col'}, dimensions={0}, use_global_device_ids=true | all-gather | bytes 52224 | tf_op jit(solution)/shard_map/while/body/eval_jaxpr/all_gather | solution.py:67
  518.2 6.4 fusion.33
  524.7 0.7 pad_maximum_fusion.2
  525.5 15.4 %all-reduce.5.cloned.1.call-done = bf16[4,2,128,128]{2,3,0,1:T(8,128)(2,1)} async-done(((bf16[4,2,128,128]{2,3,0,1:T(8,128)(2,1)}), bf16[4,2,128,128]{2,3,0,1:T(8,128)(2,1)}) %all-reduce.5.cloned.1.call-update) | async-done | bytes 262160 | tf_op jit(solution)/shard_map/while/body/eval_jaxpr/psum | solution.py:17
  540.9 1.0 multiply_convert_fusion.2
  542.0 6.8 multiply_reduce_fusion.4
  548.8 1.7 copy.28
  550.4 127.5 %reduce-scatter.6.cloned.1.call-done = f32[192,4]{1,0:T(8,128)} async-done(((f32[3072,4]{1,0:T(8,128)}), f32[192,4]{1,0:T(8,128)}) %reduce-scatter.6.cloned.1.call-update) | async-done | bytes 3088 | tf_op jit(solution)/shard_map/while
  677.9 1.0 copy.29
  679.5 40.0 %psum.25 = f32[]{:T(128)} all-reduce(f32[]{:T(128)} %multiply_reduce_fusion.5), channel_id=1, replica_groups=mesh['row'=4,'col'=4,'pts'=2] {'row','col','pts'}, use_global_device_ids=true, to_apply=%region_6.6 | all-reduce | flops 1 | bytes 8 | tf_op jit(solution)/shard_map/while/body/eval_jaxpr/psum | solution.py:21
  (36 shorter events, 2.8 us)
Async XLA Ops:
  6.5 231.6 %all-reduce.3.cloned.1.call-start = ((), (), s32[]{:S(2)}) async-start(), calls=%async_computation.1 | async-start | bytes 12582912 | tf_op jit(solution)/shard_map/psum | solution.py:13
  12.4 1.0 copy-start
  12.4 1.2 copy-start.3
  12.4 225.8 %copy-start.2 = (f32[1,4,192]{2,1,0:T(4,128)S(1)}, f32[1,4,192]{2,1,0:T(4,128)}, u32[]{:S(2)}) copy-start(f32[1,4,192]{2,1,0:T(4,128)} %param.7) | copy-start | bytes 9220
  238.1 61.0 %all-reduce.5.cloned.1.call-start = ((), (), s32[]{:S(2)}) async-start(), calls=%async_computation.2 | async-start | bytes 524288 | tf_op jit(solution)/shard_map/while/body/eval_jaxpr/psum | solution.py:17
  284.5 151.8 %reduce-scatter.6.cloned.1.call-start = ((), (), s32[]{:S(2)}) async-start(), calls=%async_computation.3 | async-start | bytes 1671168 | tf_op jit(solution)/shard_map/while
  478.6 62.3 %all-reduce.5.cloned.1.call-start = ((), (), s32[]{:S(2)}) async-start(), calls=%async_computation.2 | async-start | bytes 524288 | tf_op jit(solution)/shard_map/while/body/eval_jaxpr/psum | solution.py:17
  525.4 152.5 %reduce-scatter.6.cloned.1.call-start = ((), (), s32[]{:S(2)}) async-start(), calls=%async_computation.3 | async-start | bytes 1671168 | tf_op jit(solution)/shard_map/while
  720.2 0.6 copy-start.1
Sparse Core Ops, SparseCore 0:
  12.5 225.5 all-reduce.2
  284.6 14.5 all-reduce.4
  308.9 127.3 reduce-scatter.5
  525.5 15.2 all-reduce.4
  550.6 127.3 reduce-scatter.5
where the time goes:
time: 728 us; the launch traced here: 727 us
  waiting for transfers between devices  510 us (70%)
  blocking collectives  158 us (22%)
  matrix products  26.4 us (4%)
  between operations  13.1 us (2%)
  other arithmetic  10.9 us (1%)
  local copies, waits for them, and re-layouts  7.41 us (1%)
    while x6, waiting for transfers between devices  255 us
    psum x1, waiting for transfers between devices, from_root(): return lax.psum(block, axis)  224 us
    psum x2, blocking collectives, descend(): squares = lax.psum(jnp.sum(gradient * gradient), ('row', 'col', 'pts'))  80.1 us
    all_gather x2, blocking collectives, run_sweep(): whole_log = lax.all_gather(log_field, ('row', 'col'), axis=1, tiled=True)  78.4 us
    psum x2, waiting for transfers between devices, pair_total(): lax.psum(partial_value.astype(jnp.bfloat16), 'pts').astype(jnp.float32)  30 us
  transfers between devices with their start and end apart: 5, of which 5 were waited for; matrix products, arithmetic and copies ran while one was open for 0% of the time, Pallas kernels for 0%

commit v1 on v0

--- a/solution.py
+++ b/solution.py
@@ -8,13 +8,19 @@
 descent = 0.1
 
 
+def _trace_case(content):
+    last = lax.all_gather(content, axis_name="pts")
+    mat_out = jnp.sum(last, axis=0)
+    return mat_out
+
+
 def from_root(block, axis, source):
     block = jnp.where(lax.axis_index(axis) == source, block, jnp.zeros_like(block))
     return lax.psum(block, axis)
 
 
 def pair_total(partial_value):
-    return lax.psum(partial_value.astype(jnp.bfloat16), "pts").astype(jnp.float32)
+    return _trace_case(partial_value.astype(jnp.bfloat16)).astype(jnp.float32)
 
 
 def descend(log_field, gradient, entry_count):

time: 728 us -> 690 us (0.948)
  waiting for transfers between devices: 510 us -> 470 us
    psum x2 -> x0, waiting for transfers between devices: 30 us -> none  [pair_total(): lax.psum(partial_value.astype(jnp.bfloat16), 'pts').astype(jnp.float32)]
    while x6 -> x4, waiting for transfers between devices: 255 us -> 246 us
  transfers between devices with their start and end apart: 5 -> 3, of which waited for: 5 -> 3; matrix products, arithmetic and copies ran while one was open for 0% -> 0% of each run, Pallas kernels for 0% -> 0%
where the time goes in v1:
time: 690 us; the launch traced here: 689 us
  waiting for transfers between devices  470 us (68%)
  blocking collectives  163 us (24%)
  matrix products  25.8 us (4%)
  between operations  13.1 us (2%)
  other arithmetic  7.81 us (1%)
  local copies, waits for them, and re-layouts  7.51 us (1%)
    while x4, waiting for transfers between devices  246 us
    psum x1, waiting for transfers between devices, from_root(): return lax.psum(block, axis)  225 us
    psum x2, blocking collectives, descend(): squares = lax.psum(jnp.sum(gradient * gradient), ('row', 'col', 'pts'))  80.1 us
    all_gather x2, blocking collectives, run_sweep(): whole_log = lax.all_gather(log_field, ('row', 'col'), axis=1, tiled=True)  78.4 us
  transfers between devices with their start and end apart: 3, of which 3 were waited for; matrix products, arithmetic and copies ran while one was open for 0% of the time, Pallas kernels for 0%

profile of v1, /device:TPU:0, one launch (start us, length us, event | category | flops | bytes accessed | tf_op | source)
XLA Modules:
  0.0 689.1 jit_solution(1262105276398051565)
XLA Ops:
  6.5 5.8 broadcast_select_fusion
  12.4 1.0 copy-done
  13.5 224.7 %all-reduce.2.cloned.1.call-done = bf16[4,256,3072]{2,1,0:T(8,128)(2,1)} async-done(((bf16[4,256,3072]{2,1,0:T(8,128)(2,1)}), bf16[4,256,3072]{2,1,0:T(8,128)(2,1)}) %all-reduce.2.cloned.1.call-update) | async-done | bytes 6291472 | tf_op jit(solution)/shard_map/psum | solution.py:19
  238.1 443.8 %while.12 = (s32[]{:T(128)}, f32[4,192]{1,0:T(4,128)S(1)}, bf16[4,256,3072]{2,1,0:T(8,128)(2,1)}, f32[128,128]{1,0:T(8,128)S(1)}, bf16[4,2,128,3072]{3,2,1,0:T(8...) while((s32[]{:T(128)}, f32[4,192]{1,0:T(4,128)S(1)}, ...), condition=%wide.region_7.8_spmd, body=%wide.region_1.7_spmd.sunk | while | flops 3243458304 | bytes 34827464 | solution.py:84
  238.2 39.0 %all-gather.2 = f32[16,192,4]{1,2,0:T(4,128)S(1)} all-gather(f32[1,192,4]{1,2,0:T(4,128)S(1)} %bitcast.59), channel_id=1, replica_groups=mesh['row'=4,'col'=4,'pts'=2] {'row','col'}, dimensions={0}, use_global_device_ids=true | all-gather | bytes 52224 | tf_op jit(solution)/shard_map/while/body/eval_jaxpr/all_gather | solution.py:73
  277.2 6.4 fusion.33
  283.8 0.2 copy.34
  284.0 2.2 all_gather.14
  286.4 6.4 multiply_reduce_fusion.4
  292.9 1.7 copy.35
  294.6 122.6 %reduce-scatter.6.cloned.1.call-done = f32[192,4]{1,0:T(8,128)} async-done(((f32[3072,4]{1,0:T(8,128)}), f32[192,4]{1,0:T(8,128)}) %reduce-scatter.6.cloned.1.call-update) | async-done | bytes 3088 | tf_op jit(solution)/shard_map/while
  417.2 1.0 copy.36
  418.1 0.6 multiply_reduce_fusion.5
  418.7 40.1 %psum.19 = f32[]{:T(128)} all-reduce(f32[]{:T(128)} %multiply_reduce_fusion.5), channel_id=1, replica_groups=mesh['row'=4,'col'=4,'pts'=2] {'row','col','pts'}, use_global_device_ids=true, to_apply=%region_6.6 | all-reduce | flops 1 | bytes 8 | tf_op jit(solution)/shard_map/while/body/eval_jaxpr/psum | solution.py:27
  459.6 39.5 %all-gather.2 = f32[16,192,4]{1,2,0:T(4,128)S(1)} all-gather(f32[1,192,4]{1,2,0:T(4,128)S(1)} %bitcast.59), channel_id=1, replica_groups=mesh['row'=4,'col'=4,'pts'=2] {'row','col'}, dimensions={0}, use_global_device_ids=true | all-gather | bytes 52224 | tf_op jit(solution)/shard_map/while/body/eval_jaxpr/all_gather | solution.py:73
  499.1 6.4 fusion.33
  505.9 2.2 all_gather.14
  508.3 6.4 multiply_reduce_fusion.4
  514.8 1.7 copy.35
  516.5 123.2 %reduce-scatter.6.cloned.1.call-done = f32[192,4]{1,0:T(8,128)} async-done(((f32[3072,4]{1,0:T(8,128)}), f32[192,4]{1,0:T(8,128)}) %reduce-scatter.6.cloned.1.call-update) | async-done | bytes 3088 | tf_op jit(solution)/shard_map/while
  639.7 1.0 copy.36
  640.6 0.6 multiply_reduce_fusion.5
  641.3 40.0 %psum.19 = f32[]{:T(128)} all-reduce(f32[]{:T(128)} %multiply_reduce_fusion.5), channel_id=1, replica_groups=mesh['row'=4,'col'=4,'pts'=2] {'row','col','pts'}, use_global_device_ids=true, to_apply=%region_6.6 | all-reduce | flops 1 | bytes 8 | tf_op jit(solution)/shard_map/while/body/eval_jaxpr/psum | solution.py:27
  681.9 0.6 copy-done.1
  (35 shorter events, 1.3 us)
Async XLA Ops:
  6.5 231.6 %all-reduce.2.cloned.1.call-start = ((), (), s32[]{:S(2)}) async-start(), calls=%async_computation.1 | async-start | bytes 12582912 | tf_op jit(solution)/shard_map/psum | solution.py:19
  12.4 1.0 copy-start
  12.4 1.1 copy-start.3
  12.4 225.8 %copy-start.2 = (f32[1,4,192]{2,1,0:T(4,128)S(1)}, f32[1,4,192]{2,1,0:T(4,128)}, u32[]{:S(2)}) copy-start(f32[1,4,192]{2,1,0:T(4,128)} %param.7) | copy-start | bytes 9220
  238.1 179.0 %reduce-scatter.6.cloned.1.call-start = ((), (), s32[]{:S(2)}) async-start(), calls=%async_computation.2 | async-start | bytes 1671168 | tf_op jit(solution)/shard_map/while
  459.5 180.2 %reduce-scatter.6.cloned.1.call-start = ((), (), s32[]{:S(2)}) async-start(), calls=%async_computation.2 | async-start | bytes 1671168 | tf_op jit(solution)/shard_map/while
  681.9 0.6 copy-start.1
Sparse Core Ops, SparseCore 0:
  12.5 225.5 all-reduce.1
  294.7 122.4 reduce-scatter.5
  516.6 123.0 reduce-scatter.5
